TPU v7x, 256 devices: a whole 4x4x8 slice. The times are simulated.
256 devices in a mesh: batch: 16 (over z, core), wx: 4 (over y), wy: 4 (over x).
Axes of the slice: x: 4, y: 4, z: 8, core: 2. Of those that a mesh axis runs over, the one named last changes fastest.
Arguments:
- tokens: bfloat16 [8192, 16384], P(('batch', 'wx'), 'wy'), may hold values from -6 to 6
- routes: int32 [8192, 1], P(('batch', 'wx')), may hold values from 0 to 15; in each aligned block of 128 rows (0 to 127, 128 to 255, ...) at most 16 rows name the same one
- gate_weight: bfloat16 [16384, 2048], P('wy', 'wx'), may hold values from -0.046875 to 0.046875
- up_weight: bfloat16 [16384, 2048], P('wy', 'wx'), may hold values from -0.046875 to 0.046875
Outputs:
- hidden: bfloat16 [16384, 2048], P(('batch', 'wy'), 'wx')
Inputs may be any that keep to these rules, and one draw needn't show every extreme that they name: `routes`: among the tokens of one device, at most 16 share a group.
All inputs are finite; a program needn't handle non-finite values.
Results may differ from a plain program's by a relative error of at most 0.001.
Values may be sent and summed in bfloat16 or wider, within the bound.
No kernel may reach another device: no remote copies, remote signals or barrier semaphores. Data moves between devices by JAX's collectives and lax.ppermute only.
A program may use at most 128 MiB of HBM per device.

v0:
```python
import jax
import jax.numpy as jnp
from jax import lax
from jax.sharding import PartitionSpec as P


def place_rows(source, group_of, slots, groups_total):
    onehot = (group_of[:, None] == jnp.arange(groups_total, dtype=jnp.int32)[None, :]).astype(
        jnp.int32
    )
    ordinal = jnp.sum((jnp.cumsum(onehot, axis=0) - onehot) * onehot, axis=1)
    target = group_of * slots + ordinal
    chooser = (
        target[:, None] == jnp.arange(groups_total * slots, dtype=jnp.int32)[None, :]
    ).astype(jnp.bfloat16)
    placed = lax.dot_general(
        chooser, source, (((0,), (0,)), ((), ())), preferred_element_type=jnp.float32
    )
    return placed.astype(jnp.bfloat16)


def per_device(tokens, routes, gate_weight, up_weight):
    row_count = tokens.shape[0]
    hid = gate_weight.shape[1]
    groups_total = lax.axis_size("batch")
    wx_count = lax.axis_size("wx")
    slots = 2 * row_count // groups_total
    gathered = lax.all_gather(tokens, "wx", axis=0, tiled=True)
    group_all = lax.all_gather(routes, "wx", axis=0, tiled=True)
    gate = jnp.dot(gathered, gate_weight, preferred_element_type=jnp.float32)
    up = jnp.dot(gathered, up_weight, preferred_element_type=jnp.float32)
    both = jnp.concatenate([gate, up], axis=1)
    summed = lax.psum_scatter(both, "wy", scatter_dimension=0, tiled=True)
    gate_sum, up_sum = (summed[:, :hid], summed[:, hid:])
    hidden = (jax.nn.silu(gate_sum) * up_sum).astype(jnp.bfloat16)
    own = lax.axis_index("wy")
    group_of = lax.dynamic_slice_in_dim(group_all.reshape(wx_count, row_count), own, 1, 0)[0]
    placed = place_rows(hidden, group_of, slots, groups_total)
    placed = placed.reshape(groups_total, slots, hid)
    arrived = lax.all_to_all(placed, "batch", split_axis=0, concat_axis=0, tiled=True)
    return arrived.reshape(groups_total * slots, hid)


def solution(mesh):
    placed = (P(("batch", "wx"), "wy"), P(("batch", "wx"), None), P("wy", "wx"), P("wy", "wx"))
    return jax.shard_map(
        per_device, mesh=mesh, in_specs=placed, out_specs=P(("batch", "wy"), "wx"), check_vma=False
    )
```

profile of v0, /device:TPU:1, one launch (start us, length us, event | category | flops | bytes accessed | tf_op | source)
XLA Modules:
  0.0 134.4 jit_solution(3706500899102372639)
XLA Ops:
  6.5 0.0 all-gather.2.cloned.1.call-start
  6.5 0.7 all-gather.2.cloned.1.call-update
  7.3 0.0 reduce-scatter.2.cloned.1.call-start
  7.3 56.3 %all-gather.2.cloned.1.call-done = bf16[512,4096]{1,0:T(8,128)(2,1)} async-done(((bf16[128,4096]{1,0:T(8,128)(2,1)}), bf16[512,4096]{1,0:T(8,128)(2,1)}) %all-gather.2.cloned.1.call-update) | async-done | bytes 4194320 | tf_op jit(solution)/shard_map/all_gather | solution.py:28
  63.6 0.0 copy-start.1
  63.6 0.0 copy-start.2
  63.6 6.0 %fusion.8 = f32[512,512]{0,1:T(8,128)S(1)} fusion(bf16[512,4096]{1,0:T(8,128)(2,1)} %all-gather.2.cloned.1.call-done, bf16[4096,512]{1,0:T(8,128)(2,1)} %param.7), kind=kOutput, calls=%fused_computation.14 | convolution fusion | flops 2147483648 | bytes 9437184 | tf_op jit(solution)/shard_map/dot_general | solution.py:31
  69.6 0.0 copy-done.1
  69.6 0.0 copy-done.2
  69.6 2.4 %fusion.7 = f32[512,512]{0,1:T(8,128)S(1)} fusion(bf16[512,4096]{1,0:T(8,128)(2,1)S(1)} %copy-done.2, bf16[4096,512]{1,0:T(8,128)(2,1)S(1)} %copy-done.1), kind=kOutput, calls=%fused_computation.13 | convolution fusion | flops 2147483648 | bytes 9437184 | tf_op jit(solution)/shard_map/dot_general | solution.py:30
  72.0 0.0 copy-start
  72.0 1.5 %pad_maximum_fusion = f32[512,1024]{0,1:T(8,128)} fusion(f32[512,512]{0,1:T(8,128)S(1)} %fusion.8, f32[512,512]{0,1:T(8,128)S(1)} %fusion.7), kind=kLoop, calls=%fused_computation | loop fusion | flops 524288 | bytes 4194304 | tf_op jit(solution)/shard_map/concatenate | solution.py:32
  73.5 0.0 reduce-scatter.2.cloned.1.call-update
  73.5 0.0 copy-done
  73.5 5.8 %all_gather.6 = s32[512,1]{0,1:T(1,128)S(1)} all-gather(s32[128,1]{0,1:T(1,128)S(1)} %copy-done), channel_id=1, replica_groups=mesh['batch'=16,'wx'=4,'wy'=4] {'wx'}, dimensions={0}, use_global_device_ids=true | all-gather | bytes 2560 | tf_op jit(solution)/shard_map/all_gather | solution.py:29
  79.3 0.1 fusion.5
  79.4 0.2 reduce_window_sum.11
  79.6 0.2 select_reduce_fusion
  79.8 26.6 %reduce-scatter.2.cloned.1.call-done = f32[128,1024]{0,1:T(8,128)} async-done(((f32[512,1024]{0,1:T(8,128)}), f32[128,1024]{0,1:T(8,128)}) %reduce-scatter.2.cloned.1.call-update) | async-done | bytes 524304 | tf_op jit(solution)/shard_map/reduce_scatter | solution.py:33
  106.3 1.3 %convolution_convert_fusion = bf16[256,512]{1,0:T(8,128)(2,1)S(1)} fusion(f32[128,1024]{0,1:T(8,128)} %reduce-scatter.2.cloned.1.call-done, s32[128]{0:T(128)S(1)} %multiply_add_fusion), kind=kOutput, calls=%fused_computation.1 | convolution fusion | flops 34144256 | bytes 786944 | tf_op jit(solution)/shard_map/dot_general | solution.py:16
  107.7 19.1 %all_to_all.5 = bf16[16,16,512]{2,1,0:T(8,128)(2,1)S(1)} all-to-all(bf16[16,16,512]{2,1,0:T(8,128)(2,1)S(1)} %bitcast.12), channel_id=1, replica_groups=mesh['batch'=16,'wx'=4,'wy'=4] {'batch'}, dimensions={0} | all-to-all | bytes 524288 | tf_op jit(solution)/shard_map/all_to_all | solution.py:40
  126.8 0.7 copy.6
  (2 shorter events, 0.0 us)
Async XLA Ops:
  6.5 57.0 %all-gather.2.cloned.1.call-start = ((), (), s32[]{:S(2)}) async-start(), calls=%async_computation.2 | async-start | bytes 5242880 | tf_op jit(solution)/shard_map/all_gather | solution.py:28
  7.3 99.1 %reduce-scatter.2.cloned.1.call-start = ((), (), s32[]{:S(2)}) async-start(), calls=%async_computation.3 | async-start | bytes 2621440 | tf_op jit(solution)/shard_map/reduce_scatter | solution.py:33
  63.6 6.0 %copy-start.1 = (bf16[4096,512]{1,0:T(8,128)(2,1)S(1)}, bf16[4096,512]{1,0:T(8,128)(2,1)}, u32[]{:S(2)}) copy-start(bf16[4096,512]{1,0:T(8,128)(2,1)} %param.6) | copy-start | bytes 12582916
  63.6 6.0 %copy-start.2 = (bf16[512,4096]{1,0:T(8,128)(2,1)S(1)}, bf16[512,4096]{1,0:T(8,128)(2,1)}, u32[]{:S(2)}) copy-start(bf16[512,4096]{1,0:T(8,128)(2,1)} %all-gather.2.cloned.1.call-done) | copy-start | bytes 12582916
  72.0 1.6 %copy-start = (s32[128,1]{0,1:T(1,128)S(1)}, s32[128,1]{0,1:T(1,128)}, u32[]{:S(2)}) copy-start(s32[128,1]{0,1:T(1,128)} %param.5) | copy-start | bytes 1540
Sparse Core Ops, SparseCore 0:
  9.1 54.3 all-gather.1
  73.6 32.6 reduce-scatter.1
where the time goes:
time: 135 us; the launch traced here: 134 us
  waiting for transfers between devices  83.6 us (62%)
  blocking collectives  24.9 us (18%)
  between operations  13.5 us (10%)
  matrix products  9.68 us (7%)
  other arithmetic  1.96 us (1%)
    all_gather x1, waiting for transfers between devices, per_device(): gathered = lax.all_gather(tokens, 'wx', axis=0, tiled=True)  56.3 us
    reduce_scatter x1, waiting for transfers between devices, per_device(): summed = lax.psum_scatter(both, 'wy', scatter_dimension=0, tiled=True)  26.6 us
    all_to_all x1, blocking collectives, per_device(): lax.all_to_all(placed, 'batch', split_axis=0, concat_axis=0, tiled=True)  19.1 us
    dot_general x1, matrix products, per_device(): up = jnp.dot(gathered, up_weight, preferred_element_type=jnp.float32)  5.97 us
    all_gather x1, blocking collectives, per_device(): group_all = lax.all_gather(routes, 'wx', axis=0, tiled=True)  5.78 us
  transfers between devices with their start and end apart: 2, of which 2 were waited for; matrix products, arithmetic and copies ran while one was open for 0% of the time, Pallas kernels for 0%

commit v1 on v0

--- a/solution.py
+++ b/solution.py
@@ -25,7 +25,9 @@
     groups_total = lax.axis_size("batch")
     wx_count = lax.axis_size("wx")
     slots = 2 * row_count // groups_total
-    gathered = lax.all_gather(tokens, "wx", axis=0, tiled=True)
+    gathered = jnp.concatenate(
+        lax.all_to_all(jnp.stack([tokens for _ in range(lax.axis_size("wx"))]), "wx", 0, 0), axis=0
+    )
     group_all = lax.all_gather(routes, "wx", axis=0, tiled=True)
     gate = jnp.dot(gathered, gate_weight, preferred_element_type=jnp.float32)
     up = jnp.dot(gathered, up_weight, preferred_element_type=jnp.float32)

time: 135 us -> 130 us (0.963)
  waiting for transfers between devices: 83.6 us -> 27.8 us
  blocking collectives: 24.9 us -> 78.3 us
  matrix products: 9.68 us -> 6.08 us
  local copies, waits for them, and re-layouts: 0.72 us -> 2.44 us
    all_gather x1 -> x0, waiting for transfers between devices: 56.3 us -> none  [per_device(): gathered = lax.all_gather(tokens, 'wx', axis=0, tiled=True)]
    all_to_all x0 -> x1, blocking collectives: none -> 53 us  [per_device(): lax.all_to_all(jnp.stack([tokens for _ in range(lax.axis_size('wx'))]), '...]
    dot_general x1, matrix products: 5.97 us -> 2.37 us  [per_device(): up = jnp.dot(gathered, up_weight, preferred_element_type=jnp.float32)]
    another operation x0 -> x1, local copies, waits for them, and re-layouts: none -> 1.72 us  [per_device(): jnp.stack([tokens for _ in range(lax.axis_size('wx'))])]
  transfers between devices with their start and end apart: 2 -> 1, of which waited for: 2 -> 1; matrix products, arithmetic and copies ran while one was open for 0% -> 0% of each run, Pallas kernels for 0% -> 0%
where the time goes in v1:
time: 130 us
  blocking collectives  78.3 us (60%)
  waiting for transfers between devices  27.8 us (21%)
  between operations  13.5 us (10%)
  matrix products  6.08 us (5%)
  local copies, waits for them, and re-layouts  2.44 us (2%)
  other arithmetic  1.96 us (2%)
    all_to_all x1, blocking collectives, per_device(): lax.all_to_all(jnp.stack([tokens for _ in range(lax.axis_size('wx'))]), '...  53 us
    reduce_scatter x1, waiting for transfers between devices, per_device(): summed = lax.psum_scatter(both, 'wy', scatter_dimension=0, tiled=True)  27.8 us
    all_to_all x1, blocking collectives, per_device(): lax.all_to_all(placed, 'batch', split_axis=0, concat_axis=0, tiled=True)  19.1 us
    all_gather x1, blocking collectives, per_device(): group_all = lax.all_gather(routes, 'wx', axis=0, tiled=True)  6.11 us
  transfers between devices with their start and end apart: 1, of which 1 were waited for; matrix products, arithmetic and copies ran while one was open for 0% of the time, Pallas kernels for 0%

profile of v1, /device:TPU:1, one launch (start us, length us, event | category | flops | bytes accessed | tf_op | source)
XLA Modules:
  0.0 130.1 jit_solution(16882946619607163542)
XLA Ops:
  6.5 0.0 reduce-scatter.2.cloned.1.call-start
  6.5 1.7 %stack.2 = bf16[4,128,4096]{2,1,0:T(8,128)(2,1)S(1)} broadcast(bf16[128,4096]{1,0:T(8,128)(2,1)} %param.4), dimensions={1,2} | broadcast | bytes 5242880 | tf_op jit(solution)/shard_map/stack | solution.py:29
  8.3 0.0 copy-start.1
  8.3 53.0 %all_to_all.10 = bf16[4,128,4096]{2,1,0:T(8,128)(2,1)S(1)} all-to-all(bf16[4,128,4096]{2,1,0:T(8,128)(2,1)S(1)} %stack.2), channel_id=1, replica_groups=mesh['batch'=16,'wx'=4,'wy'=4] {'wx'}, dimensions={0} | all-to-all | bytes 8388608 | tf_op jit(solution)/shard_map/all_to_all | solution.py:29
  61.3 0.0 copy-done.1
  61.3 0.0 copy-start.2
  61.3 2.4 %fusion.8 = f32[512,512]{0,1:T(8,128)S(1)} fusion(bf16[512,4096]{1,0:T(8,128)(2,1)S(1)} %bitcast.12, bf16[4096,512]{1,0:T(8,128)(2,1)S(1)} %copy-done.1), kind=kOutput, calls=%fused_computation.14 | convolution fusion | flops 2147483648 | bytes 9437184 | tf_op jit(solution)/shard_map/dot_general | solution.py:33
  63.7 0.0 copy-done.2
  63.7 2.4 %fusion.7 = f32[512,512]{0,1:T(8,128)S(1)} fusion(bf16[512,4096]{1,0:T(8,128)(2,1)S(1)} %bitcast.13, bf16[4096,512]{1,0:T(8,128)(2,1)S(1)} %copy-done.2), kind=kOutput, calls=%fused_computation.13 | convolution fusion | flops 2147483648 | bytes 9437184 | tf_op jit(solution)/shard_map/dot_general | solution.py:32
  66.0 0.0 copy-start
  66.1 1.5 %pad_maximum_fusion = f32[512,1024]{0,1:T(8,128)} fusion(f32[512,512]{0,1:T(8,128)S(1)} %fusion.8, f32[512,512]{0,1:T(8,128)S(1)} %fusion.7), kind=kLoop, calls=%fused_computation | loop fusion | flops 524288 | bytes 4194304 | tf_op jit(solution)/shard_map/concatenate | solution.py:34
  67.6 0.0 reduce-scatter.2.cloned.1.call-update
  67.6 0.0 copy-done
  67.6 6.1 %all_gather.3 = s32[512,1]{0,1:T(1,128)S(1)} all-gather(s32[128,1]{0,1:T(1,128)S(1)} %copy-done), channel_id=1, replica_groups=mesh['batch'=16,'wx'=4,'wy'=4] {'wx'}, dimensions={0}, use_global_device_ids=true | all-gather | bytes 2560 | tf_op jit(solution)/shard_map/all_gather | solution.py:31
  73.7 0.1 fusion.5
  73.8 0.2 reduce_window_sum.11
  74.0 0.2 select_reduce_fusion
  74.2 27.8 %reduce-scatter.2.cloned.1.call-done = f32[128,1024]{0,1:T(8,128)} async-done(((f32[512,1024]{0,1:T(8,128)}), f32[128,1024]{0,1:T(8,128)}) %reduce-scatter.2.cloned.1.call-update) | async-done | bytes 524304 | tf_op jit(solution)/shard_map/reduce_scatter | solution.py:35
  102.0 1.3 %convolution_convert_fusion = bf16[256,512]{1,0:T(8,128)(2,1)S(1)} fusion(f32[128,1024]{0,1:T(8,128)} %reduce-scatter.2.cloned.1.call-done, s32[128]{0:T(128)S(1)} %multiply_add_fusion), kind=kOutput, calls=%fused_computation.1 | convolution fusion | flops 34144256 | bytes 786944 | tf_op jit(solution)/shard_map/dot_general | solution.py:16
  103.4 19.1 %all_to_all.11 = bf16[16,16,512]{2,1,0:T(8,128)(2,1)S(1)} all-to-all(bf16[16,16,512]{2,1,0:T(8,128)(2,1)S(1)} %bitcast.15), channel_id=1, replica_groups=mesh['batch'=16,'wx'=4,'wy'=4] {'batch'}, dimensions={0} | all-to-all | bytes 524288 | tf_op jit(solution)/shard_map/all_to_all | solution.py:42
  122.5 0.7 copy.6
  (2 shorter events, 0.0 us)
Async XLA Ops:
  6.5 95.5 %reduce-scatter.2.cloned.1.call-start = ((), (), s32[]{:S(2)}) async-start(), calls=%async_computation.3 | async-start | bytes 2621440 | tf_op jit(solution)/shard_map/reduce_scatter | solution.py:35
  8.3 53.0 %copy-start.1 = (bf16[4096,512]{1,0:T(8,128)(2,1)S(1)}, bf16[4096,512]{1,0:T(8,128)(2,1)}, u32[]{:S(2)}) copy-start(bf16[4096,512]{1,0:T(8,128)(2,1)} %param.7) | copy-start | bytes 12582916
  61.3 2.4 %copy-start.2 = (bf16[4096,512]{1,0:T(8,128)(2,1)S(1)}, bf16[4096,512]{1,0:T(8,128)(2,1)}, u32[]{:S(2)}) copy-start(bf16[4096,512]{1,0:T(8,128)(2,1)} %param.6) | copy-start | bytes 12582916
  66.0 1.6 %copy-start = (s32[128,1]{0,1:T(1,128)S(1)}, s32[128,1]{0,1:T(1,128)}, u32[]{:S(2)}) copy-start(s32[128,1]{0,1:T(1,128)} %param.5) | copy-start | bytes 1540
Sparse Core Ops, SparseCore 0:
  67.7 34.2 reduce-scatter.1
